TPU v7x, 256 devices: a whole 4x4x8 slice. The times are simulated.
256 devices in a mesh: grp: 8 (over x, core), cell: 32 (over y, z).
Axes of the slice: x: 4, y: 4, z: 8, core: 2. Of those that a mesh axis runs over, the one named last changes fastest.
Arguments:
- rhs: float32 [128, 2, 128, 16, 128], P('grp', None, 'cell'), may hold values from -8 to 8
- log_perm: float32 [128, 128, 16, 128], P('grp', 'cell'), may hold values from -1.5 to 1.5
- porosity: float32 [128, 128, 16, 128], P('grp', 'cell'), may hold values from 0.1 to 0.3
- saturation: float32 [128, 128, 16, 128], P('grp', 'cell'), may hold values from 0.2 to 0.8
- pressure: float32 [128, 128, 16, 128], P('grp', 'cell'), may hold values from -6 to 6
- obs_values: float32 [256], replicated, may hold values from -6 to 6
- obs_error: float32 [256], replicated, may hold values from 0.1 to 1
- noise: float32 [128, 256], replicated, may hold values from -6 to 6
- well_cell: int32 [128], replicated, may hold values from 0 to 262143
- obs_well: int32 [256], replicated, may hold values from 0 to 127
Outputs:
- increment: float32 [128, 2, 128, 16, 128], P('grp', None, 'cell')
- log_perm_post: float32 [128, 128, 16, 128], P('grp', 'cell')
- porosity_post: float32 [128, 128, 16, 128], P('grp', 'cell')
All inputs are finite; a program needn't handle non-finite values.
Results may differ from a plain program's by a relative error of at most 0.0003.
Values sent between devices are 32-bit elements; how exact they have to be, the bound alone decides.
No kernel may reach another device: no remote copies, remote signals or barrier semaphores. Data moves between devices by JAX's collectives and lax.ppermute only.
A program may use at most 128 MiB of HBM per device.

v0:
```python
import math
import jax
import jax.numpy as jnp
from jax import lax
from jax.sharding import Mesh
from jax.sharding import PartitionSpec as P

KRYLOV = 4
epsilon = 1e-06
time_step = 0.1
compress = 0.5
inflation = 4.0
CELL = ("cy", "cz")


def cell_sum(values, doubling=False):
    for axis in ("cz", "cy"):
        size = lax.axis_size(axis)
        if not doubling or size & size - 1:
            values = lax.psum(values, axis)
            continue
        step = 1
        while step < size:
            values = values + lax.ppermute(values, axis, [(i, i ^ step) for i in range(size)])
            step *= 2
    return values


def with_halo(block, sides, width):
    for axis, dim in sides:
        count = lax.axis_size(axis[0]) * lax.axis_size(axis[1])
        forward = [(i, i + 1) for i in range(count - 1)]
        backward = [(target, source) for source, target in forward]
        low = lax.ppermute(
            lax.slice_in_dim(block, block.shape[dim] - width, None, axis=dim), axis, forward
        )
        high = lax.ppermute(lax.slice_in_dim(block, 0, width, axis=dim), axis, backward)
        block = jnp.concatenate([low, block, high], axis=dim)
    return block


def mobility(sat_field):
    return sat_field * sat_field + 0.5 * (1.0 - sat_field) * (1.0 - sat_field)


def face_pair(perm_low, perm_high, sat_low, sat_high):
    trans = (
        2.0
        * perm_low
        * perm_high
        / (perm_low + perm_high)
        * (0.5 * (mobility(sat_low) + mobility(sat_high)))
    )
    return (trans, trans * (0.5 * (sat_low + sat_high)))


def plane_faces(perm, sat_field):
    plane_rows = perm.shape[-2]
    plane_cols = perm.shape[-1]
    keep_rows = (
        lax.broadcasted_iota(jnp.int32, (plane_rows, plane_cols), 0) < plane_rows - 1
    ).astype(jnp.float32)
    keep_cols = (
        lax.broadcasted_iota(jnp.int32, (plane_rows, plane_cols), 1) < plane_cols - 1
    ).astype(jnp.float32)
    trans_y, frac_y = face_pair(
        perm, jnp.roll(perm, -1, -2), sat_field, jnp.roll(sat_field, -1, -2)
    )
    trans_z, frac_z = face_pair(
        perm, jnp.roll(perm, -1, -1), sat_field, jnp.roll(sat_field, -1, -1)
    )
    return (trans_y * keep_rows, frac_y * keep_rows, trans_z * keep_cols, frac_z * keep_cols)


def operator(padded, second, coeffs):
    accum, trans_x, frac_x, trans_y, frac_y, trans_z, frac_z = coeffs
    first = padded[..., 1:-1, :, :]
    diff_x = padded[..., 1:, :, :] - padded[..., :-1, :, :]
    diff_y = jnp.roll(first, -1, -2) - first
    diff_z = jnp.roll(first, -1, -1) - first

    def net(coef_x, coef_y, coef_z):
        flow_x = coef_x * diff_x
        flow_y = coef_y * diff_y
        flow_z = coef_z * diff_z
        return (
            flow_x[..., :-1, :, :]
            - flow_x[..., 1:, :, :]
            + (jnp.roll(flow_y, 1, -2) - flow_y)
            + (jnp.roll(flow_z, 1, -1) - flow_z)
        )

    out_pressure = accum * (compress * first + 0.5 * second) + net(trans_x, trans_y, trans_z)
    out_water = accum * second + net(frac_x, frac_y, frac_z)
    return (out_pressure, out_water)


def least_squares(columns, beta):
    rows = [list(column) for column in columns]
    cosines = []
    sines = []
    target = [beta] + [jnp.zeros_like(beta) for column in columns]
    for jdx in range(len(rows)):
        column = rows[jdx]
        for idx in range(jdx):
            upper = cosines[idx] * column[idx] + sines[idx] * column[idx + 1]
            column[idx + 1] = -sines[idx] * column[idx] + cosines[idx] * column[idx + 1]
            column[idx] = upper
        radius = jnp.sqrt(column[jdx] * column[jdx] + column[jdx + 1] * column[jdx + 1])
        cosines.append(column[jdx] / radius)
        sines.append(column[jdx + 1] / radius)
        column[jdx] = radius
        target[jdx + 1] = -sines[jdx] * target[jdx]
        target[jdx] = cosines[jdx] * target[jdx]
    count = len(rows)
    solved = [None] * count
    for jdx in reversed(range(count)):
        partial_sum = target[jdx]
        for idx in range(jdx + 1, count):
            partial_sum = partial_sum - rows[idx][jdx] * solved[idx]
        solved[jdx] = partial_sum / rows[jdx][jdx]
    return solved


def ensemble_weights(predicted, obs_values, obs_error, noise, offset, count):
    members = predicted.shape[0]
    sigma = math.sqrt(inflation) * obs_error
    center = jnp.mean(predicted, axis=0)
    spread = (predicted - center) / (math.sqrt(members - 1.0) * sigma)
    innov = (obs_values + sigma * noise - predicted) / sigma
    own_innov = lax.dynamic_slice_in_dim(innov, offset, count, 0)
    gram = jnp.eye(members, dtype=jnp.float32) + jnp.dot(
        spread, spread.T, precision=lax.Precision.HIGHEST, preferred_element_type=jnp.float32
    )
    cross = jnp.dot(
        spread, own_innov.T, precision=lax.Precision.HIGHEST, preferred_element_type=jnp.float32
    )
    factor = jnp.linalg.cholesky(gram)
    return jax.scipy.linalg.cho_solve((factor, True), cross)


def expand(values):
    return values[:, None, None, None, None]


def inner(left, right):
    return jnp.sum(left * right, axis=(1, 2, 3, 4))


def local(
    rhs, log_perm, porosity, saturation, pressure, obs_values, obs_error, noise, well_cell, obs_well
):
    local_members, slab_x, plane_rows, plane_cols = log_perm.shape
    members = noise.shape[0]
    plane = plane_rows * plane_cols
    cells_dev = slab_x * plane
    slab_index = lax.axis_index("cy") * lax.axis_size("cz") + lax.axis_index("cz")
    slab_count = lax.axis_size("cy") * lax.axis_size("cz")
    count = slab_count
    forward = [(i, i + 1) for i in range(count - 1)]
    backward = [(target, source) for source, target in forward]
    edges = (log_perm, saturation, rhs[:, 0])
    low = lax.ppermute(jnp.stack([field[:, -1:] for field in edges], 1), CELL, forward)
    high = lax.ppermute(jnp.stack([field[:, :1] for field in edges], 1), CELL, backward)
    perm_pad = jnp.exp(jnp.concatenate([low[:, 0], log_perm, high[:, 0]], axis=1))
    sat_pad = jnp.concatenate([low[:, 1], saturation, high[:, 1]], axis=1)
    trans_x, frac_x = face_pair(perm_pad[:, :-1], perm_pad[:, 1:], sat_pad[:, :-1], sat_pad[:, 1:])
    face_pos = lax.broadcasted_iota(jnp.int32, (slab_x + 1, 1, 1), 0)
    keep_face = jnp.where(
        face_pos == 0,
        slab_index > 0,
        jnp.where(face_pos == slab_x, slab_index < slab_count - 1, True),
    ).astype(jnp.float32)
    trans_x = trans_x * keep_face
    frac_x = frac_x * keep_face
    trans_y, frac_y, trans_z, frac_z = plane_faces(perm_pad[:, 1:-1], saturation)
    coeffs = (porosity / time_step, trans_x, frac_x, trans_y, frac_y, trans_z, frac_z)

    def planes(field):
        low = lax.ppermute(field[:, -1:], CELL, forward)
        high = lax.ppermute(field[:, :1], CELL, backward)
        return (low, high)

    def apply(vector, ghosts):
        padded = jnp.concatenate([ghosts[0], vector[:, 0], ghosts[1]], axis=1)
        out_pressure, out_water = operator(padded, vector[:, 1], coeffs)
        return jnp.stack([out_pressure, out_water], 1)

    def scale_planes(ghosts, scale):
        factor = scale[:, None, None, None]
        return (ghosts[0] / factor, ghosts[1] / factor)

    rhs_planes = (low[:, 2], high[:, 2])
    image = apply(rhs, rhs_planes)
    image_planes = planes(image[:, 0])
    reduced = cell_sum(jnp.stack([inner(rhs, rhs), inner(rhs, image)], 0))
    beta = jnp.sqrt(reduced[0] + epsilon)
    basis = [rhs / expand(beta)]
    basis_planes = [scale_planes(rhs_planes, beta)]
    image = image / expand(beta)
    image_planes = scale_planes(image_planes, beta)
    projected = [reduced[1] / (beta * beta)]
    columns = []
    for jdx in range(KRYLOV):
        ortho = image
        ortho_low, ortho_high = image_planes
        for idx in range(jdx + 1):
            ortho = ortho - expand(projected[idx]) * basis[idx]
            factor = projected[idx][:, None, None, None]
            ortho_low = ortho_low - factor * basis_planes[idx][0]
            ortho_high = ortho_high - factor * basis_planes[idx][1]
        ortho_planes = (ortho_low, ortho_high)
        if jdx == KRYLOV - 1:
            height = jnp.sqrt(cell_sum(inner(ortho, ortho)) + epsilon)
            columns.append(projected + [height])
            break
        image = apply(ortho, ortho_planes)
        image_planes = planes(image[:, 0])
        parts = [inner(ortho, ortho)]
        parts += [inner(basis[idx], image) for idx in range(jdx + 1)]
        parts.append(inner(ortho, image))
        reduced = cell_sum(jnp.stack(parts, 0))
        height = jnp.sqrt(reduced[0] + epsilon)
        columns.append(projected + [height])
        basis.append(ortho / expand(height))
        basis_planes.append(scale_planes(ortho_planes, height))
        image = image / expand(height)
        image_planes = scale_planes(image_planes, height)
        projected = [reduced[1 + idx] / height for idx in range(jdx + 1)]
        projected.append(reduced[jdx + 2] / (height * height))
    solved = least_squares(columns, beta)
    increment = expand(solved[0]) * basis[0]
    for jdx in range(1, KRYLOV):
        increment = increment + expand(solved[jdx]) * basis[jdx]
    cells = jnp.take(well_cell, obs_well)
    wells = well_cell.shape[0]
    component = (jnp.arange(obs_well.shape[0], dtype=jnp.int32) >= wells).astype(jnp.int32)
    slab_row = cells // plane - slab_index * slab_x
    inside = (slab_row >= 0) & (slab_row < slab_x)
    rows = 2 * slab_x * plane_rows
    row = component * (slab_x * plane_rows) + slab_row * plane_rows + cells % plane // plane_cols
    col_z = cells % plane_cols
    state = jnp.stack([pressure + increment[:, 0], saturation + increment[:, 1]], 1)
    table = state.reshape(local_members * rows, plane_cols)
    pick_z = lax.broadcasted_iota(jnp.int32, (plane_cols, cells.shape[0]), 0) == col_z[None, :]
    by_row = jnp.dot(
        table,
        pick_z.astype(jnp.float32),
        precision=lax.Precision.HIGHEST,
        preferred_element_type=jnp.float32,
    )
    pick_row = (
        lax.broadcasted_iota(jnp.int32, (rows, cells.shape[0]), 0) == row[None, :]
    ) & inside[None, :]
    picked = jnp.sum(
        by_row.reshape(local_members, rows, cells.shape[0]) * pick_row.astype(jnp.float32)[None],
        axis=1,
    )
    slab_pred = cell_sum(picked, doubling=True)
    predicted = lax.all_gather(slab_pred, "grp", axis=0, tiled=True)
    params = jnp.stack([log_perm, porosity], 1).reshape(local_members, 2 * cells_dev)
    offset = lax.axis_index("grp") * local_members
    own_columns = ensemble_weights(predicted, obs_values, obs_error, noise, offset, local_members)
    scale_factor = 1.0 / math.sqrt(members - 1.0)
    scaled = params * scale_factor
    update = jnp.dot(
        own_columns.T,
        lax.all_gather(scaled, "grp", axis=0, tiled=True),
        precision=lax.Precision.HIGHEST,
        preferred_element_type=jnp.float32,
    )
    posterior = params + update
    posterior = posterior.reshape(local_members, 2, slab_x, plane_rows, plane_cols)
    return (increment, posterior[:, 0], posterior[:, 1])


def split_mesh(mesh):
    devices = mesh.devices
    groups, slabs = devices.shape
    along_z = len({device.coords[2] for device in devices[0]})
    return Mesh(devices.reshape(groups, slabs // along_z, along_z), ("grp", "cy", "cz"))


def solution(mesh):
    mesh = split_mesh(mesh)
    in_specs = (
        P("grp", None, CELL, None, None),
        P("grp", CELL, None, None),
        P("grp", CELL, None, None),
        P("grp", CELL, None, None),
        P("grp", CELL, None, None),
        P(),
        P(),
        P(),
        P(),
        P(),
    )
    out_specs = (
        P("grp", None, CELL, None, None),
        P("grp", CELL, None, None),
        P("grp", CELL, None, None),
    )
    return jax.shard_map(local, mesh=mesh, in_specs=in_specs, out_specs=out_specs, check_vma=False)
```

profile of v0, /device:TPU:1, one launch (start us, length us, event | category | flops | bytes accessed | tf_op | source)
XLA Modules:
  0.0 307.5 jit_solution(6333934453051698767)
XLA Ops:
  13.3 5.0 %collective-permute-start = (f32[16,3,1,16,128]{4,3,0,2,1:T(8,128)}, f32[16,3,1,16,128]{4,3,0,2,1:T(8,128)S(1)}, u32[]{:S(2)}, u32[]{:S(2)}) collective-permute-start(f32[16,3,1,16,128]{4,3,0,2,1:T(8,128)} %pad_maximum_fusion.12), channel_id=1, source_target_pairs={{0,1},{1,2},{2,3},{3,4},{4,5},{5,6},{6,7},{7,8},{8,9},{9,10},{10,1... | collective-permute-start | bytes 1179656 | tf_op jit(solution)/shard_map/ppermute | solution.py:163
  34.1 19.3 %psum.70 = f32[2,16]{1,0:T(2,128)S(1)} all-reduce(f32[2,16]{1,0:T(2,128)S(1)} %pad_maximum_fusion.16), channel_id=1, replica_groups=mesh['grp'=8,'cy'=4,'cz'=8] {'cz'}, use_global_device_ids=true, to_apply=%region_2.3 | all-reduce | flops 32 | bytes 256 | tf_op jit(solution)/shard_map/psum | solution.py:20
  53.5 10.3 %psum.71 = f32[2,16]{1,0:T(2,128)S(1)} all-reduce(f32[2,16]{1,0:T(2,128)S(1)} %psum.70), channel_id=1, replica_groups=mesh['grp'=8,'cy'=4,'cz'=8] {'cy'}, use_global_device_ids=true, to_apply=%region_3.4 | all-reduce | flops 32 | bytes 256 | tf_op jit(solution)/shard_map/psum | solution.py:20
  65.8 4.0 %collective-permute-start.3 = (f32[16,1,16,128]{3,2,1,0:T(8,128)S(1)}, f32[16,1,16,128]{3,2,1,0:T(8,128)S(1)}, u32[]{:S(2)}, u32[]{:S(2)}) collective-permute-start(f32[16,1,16,128]{3,2,1,0:T(8,128)S(1)} %get-tuple-element.72), channel_id=1, source_target_pairs={{0,1},{1,2},{2,3},{3,4},{4,5},{5,6},{6,7},{7,8},{8,9},{9,10},{10,1... | collective-permute-start | bytes 393224 | tf_op jit(solution)/shard_map/ppermute | solution.py:180
  76.6 14.2 %psum.72 = f32[3,16]{1,0:T(4,128)S(1)} all-reduce(f32[3,16]{1,0:T(4,128)S(1)} %pad_maximum_fusion.14), channel_id=1, replica_groups=mesh['grp'=8,'cy'=4,'cz'=8] {'cz'}, use_global_device_ids=true, to_apply=%region_7.8 | all-reduce | flops 48 | bytes 384 | tf_op jit(solution)/shard_map/psum | solution.py:20
  90.9 6.0 %psum.73 = f32[3,16]{1,0:T(4,128)S(1)} all-reduce(f32[3,16]{1,0:T(4,128)S(1)} %psum.72), channel_id=1, replica_groups=mesh['grp'=8,'cy'=4,'cz'=8] {'cy'}, use_global_device_ids=true, to_apply=%region_8.9 | all-reduce | flops 48 | bytes 384 | tf_op jit(solution)/shard_map/psum | solution.py:20
  97.4 2.6 multiply_subtract_fusion.1
  101.7 4.2 %collective-permute-start.5 = (f32[16,1,16,128]{3,2,1,0:T(8,128)S(1)}, f32[16,1,16,128]{3,2,1,0:T(8,128)S(1)}, u32[]{:S(2)}, u32[]{:S(2)}) collective-permute-start(f32[16,1,16,128]{3,2,1,0:T(8,128)S(1)} %get-tuple-element.70), channel_id=1, source_target_pairs={{0,1},{1,2},{2,3},{3,4},{4,5},{5,6},{6,7},{7,8},{8,9},{9,10},{10,1... | collective-permute-start | bytes 393224 | tf_op jit(solution)/shard_map/ppermute | solution.py:180
  112.2 14.7 %psum.74 = f32[4,16]{1,0:T(4,128)} all-reduce(f32[4,16]{1,0:T(4,128)S(1)} %pad_maximum_fusion.15), channel_id=1, replica_groups=mesh['grp'=8,'cy'=4,'cz'=8] {'cz'}, use_global_device_ids=true, to_apply=%region_13.14 | all-reduce | flops 64 | bytes 512 | tf_op jit(solution)/shard_map/psum | solution.py:20
  126.9 7.4 %psum.75 = f32[4,16]{1,0:T(4,128)} all-reduce(f32[4,16]{1,0:T(4,128)} %psum.74), channel_id=1, replica_groups=mesh['grp'=8,'cy'=4,'cz'=8] {'cy'}, use_global_device_ids=true, to_apply=%region_14.15 | all-reduce | flops 64 | bytes 512 | tf_op jit(solution)/shard_map/psum | solution.py:20
  136.1 2.4 copy_subtract_fusion
  140.3 4.0 %collective-permute-start.7 = (f32[16,1,16,128]{3,2,1,0:T(8,128)S(1)}, f32[16,1,16,128]{3,2,1,0:T(8,128)S(1)}, u32[]{:S(2)}, u32[]{:S(2)}) collective-permute-start(f32[16,1,16,128]{3,2,1,0:T(8,128)S(1)} %get-tuple-element.68), channel_id=1, source_target_pairs={{0,1},{1,2},{2,3},{3,4},{4,5},{5,6},{6,7},{7,8},{8,9},{9,10},{10,1... | collective-permute-start | bytes 393224 | tf_op jit(solution)/shard_map/ppermute | solution.py:180
  149.6 14.1 %psum.76 = f32[5,16]{1,0:T(8,128)S(1)} all-reduce(f32[5,16]{1,0:T(8,128)S(1)} %stack.169), channel_id=1, replica_groups=mesh['grp'=8,'cy'=4,'cz'=8] {'cz'}, use_global_device_ids=true, to_apply=%region_20.21 | all-reduce | flops 80 | bytes 640 | tf_op jit(solution)/shard_map/psum | solution.py:20
  163.7 7.9 %psum.77 = f32[5,16]{1,0:T(8,128)S(1)} all-reduce(f32[5,16]{1,0:T(8,128)S(1)} %psum.76), channel_id=1, replica_groups=mesh['grp'=8,'cy'=4,'cz'=8] {'cy'}, use_global_device_ids=true, to_apply=%region_21.22 | all-reduce | flops 80 | bytes 640 | tf_op jit(solution)/shard_map/psum | solution.py:20
  174.0 12.3 %psum.78 = f32[16]{0:T(128)S(1)} all-reduce(f32[16]{0:T(128)S(1)} %multiply_reduce_fusion.1), channel_id=1, replica_groups=mesh['grp'=8,'cy'=4,'cz'=8] {'cz'}, use_global_device_ids=true, to_apply=%region_23.24 | all-reduce | flops 16 | bytes 128 | tf_op jit(solution)/shard_map/psum | solution.py:20
  186.3 6.1 %psum.79 = f32[16]{0:T(128)S(1)} all-reduce(f32[16]{0:T(128)S(1)} %psum.78), channel_id=1, replica_groups=mesh['grp'=8,'cy'=4,'cz'=8] {'cy'}, use_global_device_ids=true, to_apply=%region_24.25 | all-reduce | flops 16 | bytes 128 | tf_op jit(solution)/shard_map/psum | solution.py:20
  197.7 2.5 collective-permute-done.8
  200.1 3.5 %collective-permute-done.9 = f32[16,256]{1,0:T(8,128)S(1)} collective-permute-done((f32[16,256]{1,0:T(8,128)S(1)}, f32[16,256]{1,0:T(8,128)S(1)}, u32[]{:S(2)}, u32[]{:S(2)}) %collective-permute-start.9) | collective-permute-done | bytes 16416 | tf_op jit(solution)/shard_map/ppermute | solution.py:24
  205.9 4.4 %collective-permute-done.10 = f32[16,256]{1,0:T(8,128)S(1)} collective-permute-done((f32[16,256]{1,0:T(8,128)S(1)}, f32[16,256]{1,0:T(8,128)S(1)}, u32[]{:S(2)}, u32[]{:S(2)}) %collective-permute-start.10) | collective-permute-done | bytes 16416 | tf_op jit(solution)/shard_map/ppermute | solution.py:24
  213.8 3.2 %collective-permute-done.12 = f32[16,256]{1,0:T(8,128)S(1)} collective-permute-done((f32[16,256]{1,0:T(8,128)S(1)}, f32[16,256]{1,0:T(8,128)S(1)}, u32[]{:S(2)}, u32[]{:S(2)}) %collective-permute-start.12) | collective-permute-done | bytes 16416 | tf_op jit(solution)/shard_map/ppermute | solution.py:24
  217.0 50.4 %all_gather.6 = f32[128,256]{1,0:T(8,128)S(1)} all-gather(f32[16,256]{1,0:T(8,128)S(1)} %add.480), channel_id=1, replica_groups=mesh['grp'=8,'cy'=4,'cz'=8] {'grp'}, dimensions={0}, use_global_device_ids=true | all-gather | bytes 147456 | tf_op jit(solution)/shard_map/all_gather | solution.py:260
  267.9 11.7 %cholesky.17 = f32[128,128]{1,0:T(8,128)S(1)} custom-call(f32[128,128]{1,0:T(8,128)S(1)} %fusion.71), custom_call_target="Cholesky" | custom-call | tf_op jit(solution)/shard_map/jit(cholesky)/cholesky | solution.py:138
  280.9 9.8 %custom-call.10 = f32[1,128,128]{1,2,0:T(8,128)S(1)} custom-call(f32[1,128,128]{2,1,0:T(8,128)S(1)} %fusion.65), custom_call_target="InvertDiagBlocksLowerTriangular" | custom-call | tf_op jit(solution)/shard_map/jit(_cho_solve)/triangular_solve | solution.py:139
  292.3 7.1 %fusion = f32[2,8,128,128]{3,1,2,0:T(8,128)S(1)} fusion(f32[128,16]{1,0:T(8,128)S(1)} %fusion.66, f32[128,16384]{1,0:T(8,128)} %all-gather.2.cloned.1.call-done, f32[2,8,128,128]{3,2,1,0:T(8,128)S(1)} %bitcast.504), kind=kOutput, calls=%fused_computation.3 | convolution fusion | flops 402915328 | bytes 10493952 | tf_op jit(solution)/shard_map/dot_general | solution.py:266
  (265 shorter events, 65.0 us)
Async XLA Ops:
  7.2 285.1 %all-gather.2.cloned.1.call-start = ((), (), s32[]{:S(2)}) async-start(), calls=%async_computation | async-start | bytes 9437184 | tf_op jit(solution)/shard_map/all_gather | solution.py:268
  11.3 15.3 %collective-permute-start.1 = (f32[16,3,1,16,128]{4,3,0,2,1:T(8,128)}, f32[16,3,1,16,128]{4,3,0,2,1:T(8,128)S(1)}, u32[]{:S(2)}, u32[]{:S(2)}) collective-permute-start(f32[16,3,1,16,128]{4,3,0,2,1:T(8,128)} %pad_maximum_fusion.13), channel_id=1, source_target_pairs={{1,0},{2,1},{3,2},{4,3},{5,4},{6,5},{7,6},{8,7},{9,8},{10,9},{11,1... | collective-permute-start | bytes 1179656 | tf_op jit(solution)/shard_map/ppermute | solution.py:164
  13.3 13.3 %collective-permute-start = (f32[16,3,1,16,128]{4,3,0,2,1:T(8,128)}, f32[16,3,1,16,128]{4,3,0,2,1:T(8,128)S(1)}, u32[]{:S(2)}, u32[]{:S(2)}) collective-permute-start(f32[16,3,1,16,128]{4,3,0,2,1:T(8,128)} %pad_maximum_fusion.12), channel_id=1, source_target_pairs={{0,1},{1,2},{2,3},{3,4},{4,5},{5,6},{6,7},{7,8},{8,9},{9,10},{10,1... | collective-permute-start | bytes 1179656 | tf_op jit(solution)/shard_map/ppermute | solution.py:163
  25.8 80.1 %copy-start.43 = (f32[128]{0:T(128)}, f32[128]{0:T(128)S(1)}, u32[]{:S(2)}) copy-start(f32[128]{0:T(128)S(1)} %compare_convert_fusion) | copy-start | bytes 1540
  25.8 80.1 %copy-start.44 = (f32[16]{0:T(128)}, f32[16]{0:T(128)S(1)}, u32[]{:S(2)}) copy-start(f32[16]{0:T(128)S(1)} %compare_convert_fusion.1) | copy-start | bytes 196
  64.4 9.1 %collective-permute-start.2 = (f32[16,1,16,128]{3,2,1,0:T(8,128)S(1)}, f32[16,1,16,128]{3,2,1,0:T(8,128)S(1)}, u32[]{:S(2)}, u32[]{:S(2)}) collective-permute-start(f32[16,1,16,128]{3,2,1,0:T(8,128)S(1)} %get-tuple-element.71), channel_id=1, source_target_pairs={{1,0},{2,1},{3,2},{4,3},{5,4},{6,5},{7,6},{8,7},{9,8},{10,9},{11,1... | collective-permute-start | bytes 393224 | tf_op jit(solution)/shard_map/ppermute | solution.py:181
  65.8 7.7 %collective-permute-start.3 = (f32[16,1,16,128]{3,2,1,0:T(8,128)S(1)}, f32[16,1,16,128]{3,2,1,0:T(8,128)S(1)}, u32[]{:S(2)}, u32[]{:S(2)}) collective-permute-start(f32[16,1,16,128]{3,2,1,0:T(8,128)S(1)} %get-tuple-element.72), channel_id=1, source_target_pairs={{0,1},{1,2},{2,3},{3,4},{4,5},{5,6},{6,7},{7,8},{8,9},{9,10},{10,1... | collective-permute-start | bytes 393224 | tf_op jit(solution)/shard_map/ppermute | solution.py:180
  100.4 8.0 %collective-permute-start.4 = (f32[16,1,16,128]{3,2,1,0:T(8,128)S(1)}, f32[16,1,16,128]{3,2,1,0:T(8,128)S(1)}, u32[]{:S(2)}, u32[]{:S(2)}) collective-permute-start(f32[16,1,16,128]{3,2,1,0:T(8,128)S(1)} %get-tuple-element.69), channel_id=1, source_target_pairs={{1,0},{2,1},{3,2},{4,3},{5,4},{6,5},{7,6},{8,7},{9,8},{10,9},{11,1... | collective-permute-start | bytes 393224 | tf_op jit(solution)/shard_map/ppermute | solution.py:181
  101.7 6.7 %collective-permute-start.5 = (f32[16,1,16,128]{3,2,1,0:T(8,128)S(1)}, f32[16,1,16,128]{3,2,1,0:T(8,128)S(1)}, u32[]{:S(2)}, u32[]{:S(2)}) collective-permute-start(f32[16,1,16,128]{3,2,1,0:T(8,128)S(1)} %get-tuple-element.70), channel_id=1, source_target_pairs={{0,1},{1,2},{2,3},{3,4},{4,5},{5,6},{6,7},{7,8},{8,9},{9,10},{10,1... | collective-permute-start | bytes 393224 | tf_op jit(solution)/shard_map/ppermute | solution.py:180
  138.9 7.2 %collective-permute-start.6 = (f32[16,1,16,128]{3,2,1,0:T(8,128)S(1)}, f32[16,1,16,128]{3,2,1,0:T(8,128)S(1)}, u32[]{:S(2)}, u32[]{:S(2)}) collective-permute-start(f32[16,1,16,128]{3,2,1,0:T(8,128)S(1)} %get-tuple-element.67), channel_id=1, source_target_pairs={{1,0},{2,1},{3,2},{4,3},{5,4},{6,5},{7,6},{8,7},{9,8},{10,9},{11,1... | collective-permute-start | bytes 393224 | tf_op jit(solution)/shard_map/ppermute | solution.py:181
  140.3 5.9 %collective-permute-start.7 = (f32[16,1,16,128]{3,2,1,0:T(8,128)S(1)}, f32[16,1,16,128]{3,2,1,0:T(8,128)S(1)}, u32[]{:S(2)}, u32[]{:S(2)}) collective-permute-start(f32[16,1,16,128]{3,2,1,0:T(8,128)S(1)} %get-tuple-element.68), channel_id=1, source_target_pairs={{0,1},{1,2},{2,3},{3,4},{4,5},{5,6},{6,7},{7,8},{8,9},{9,10},{10,1... | collective-permute-start | bytes 393224 | tf_op jit(solution)/shard_map/ppermute | solution.py:180
  148.2 44.2 %copy-start.42 = (f32[4,16]{1,0:T(4,128)S(1)}, f32[4,16]{1,0:T(4,128)}, u32[]{:S(2)}) copy-start(f32[4,16]{1,0:T(4,128)} %psum.75) | copy-start | bytes 772
  148.2 44.2 %copy-start.46 = (f32[3,16]{1,0:T(4,128)S(1)}, f32[3,16]{1,0:T(4,128)}, u32[]{:S(2)}) copy-start(f32[3,16]{1,0:T(4,128)} %copy-done.45) | copy-start | bytes 580
  148.2 44.2 %copy-start.48 = (f32[2,16]{1,0:T(2,128)S(1)}, f32[2,16]{1,0:T(2,128)}, u32[]{:S(2)}) copy-start(f32[2,16]{1,0:T(2,128)} %copy-done.47) | copy-start | bytes 388
  148.2 44.2 %copy-start.50 = (f32[16]{0:T(128)S(1)}, f32[16]{0:T(128)}, u32[]{:S(2)}) copy-start(f32[16]{0:T(128)} %copy-done.49) | copy-start | bytes 196
  148.2 44.2 %copy-start.52 = (f32[16]{0:T(128)S(1)}, f32[16]{0:T(128)}, u32[]{:S(2)}) copy-start(f32[16]{0:T(128)} %copy-done.51) | copy-start | bytes 196
  148.2 44.2 %copy-start.55 = (f32[16]{0:T(128)S(1)}, f32[16]{0:T(128)}, u32[]{:S(2)}) copy-start(f32[16]{0:T(128)} %get-tuple-element.97) | copy-start | bytes 196
  174.0 116.8 %copy-start.57 = (f32[256]{0:T(256)S(1)}, f32[256]{0:T(256)}, u32[]{:S(2)}) copy-start(f32[256]{0:T(256)} %param.15) | copy-start | bytes 3076
  194.6 97.7 %copy-start.24 = (f32[16,2,4,16,128]{4,3,2,1,0:T(8,128)S(1)}, f32[16,2,4,16,128]{4,3,2,1,0:T(8,128)}, u32[]{:S(2)}) copy-start(f32[16,2,4,16,128]{4,3,2,1,0:T(8,128)} %copy-done.23) | copy-start | bytes 3145732
  197.5 2.7 collective-permute-start.8
  200.1 3.5 %collective-permute-start.9 = (f32[16,256]{1,0:T(8,128)S(1)}, f32[16,256]{1,0:T(8,128)S(1)}, u32[]{:S(2)}, u32[]{:S(2)}) collective-permute-start(f32[16,256]{1,0:T(8,128)S(1)} %add.476), channel_id=1, source_target_pairs={{0,2},{1,3},{2,0},{3,1},{4,6},{5,7},{6,4},{7,5},{8,10},{9,11},{10,... | collective-permute-start | bytes 49160 | tf_op jit(solution)/shard_map/ppermute | solution.py:24
  203.7 6.7 %collective-permute-start.10 = (f32[16,256]{1,0:T(8,128)S(1)}, f32[16,256]{1,0:T(8,128)S(1)}, u32[]{:S(2)}, u32[]{:S(2)}) collective-permute-start(f32[16,256]{1,0:T(8,128)S(1)} %add.477), channel_id=1, source_target_pairs={{0,4},{1,5},{2,6},{3,7},{4,0},{5,1},{6,2},{7,3},{8,12},{9,13},{10,... | collective-permute-start | bytes 49160 | tf_op jit(solution)/shard_map/ppermute | solution.py:24
  210.3 2.6 collective-permute-start.11
  212.9 4.1 %collective-permute-start.12 = (f32[16,256]{1,0:T(8,128)S(1)}, f32[16,256]{1,0:T(8,128)S(1)}, u32[]{:S(2)}, u32[]{:S(2)}) collective-permute-start(f32[16,256]{1,0:T(8,128)S(1)} %add.479), channel_id=1, source_target_pairs={{0,16},{8,24},{16,0},{24,8},{1,17},{9,25},{17,1},{25,9},{2,18},{10... | collective-permute-start | bytes 49160 | tf_op jit(solution)/shard_map/ppermute | solution.py:24
  (48 other events, 515.4 us)
Sparse Core Ops, SparseCore 0:
  22.6 56.6 all-gather.1
where the time goes:
time: 308 us
  blocking collectives  163 us (53%)
  other arithmetic  64.7 us (21%)
  starting transfers between devices  27.4 us (9%)
  between operations  15.4 us (5%)
  waiting for transfers between devices  15 us (5%)
  local copies, waits for them, and re-layouts  12.4 us (4%)
  matrix products  9.87 us (3%)
    psum x10, blocking collectives, cell_sum(): values = lax.psum(values, axis)  112 us
    all_gather x1, blocking collectives, local(): predicted = lax.all_gather(slab_pred, 'grp', axis=0, tiled=True)  50.4 us
    ppermute x5, waiting for transfers between devices, cell_sum(): lax.ppermute(values, axis, [(i, i ^ step) for i in range(size)])  14.8 us
    another operation x3, other arithmetic, ensemble_weights(): factor = jnp.linalg.cholesky(gram)  12.4 us
    ppermute x3, starting transfers between devices, planes(): low = lax.ppermute(field[:, -1:], CELL, forward)  12.2 us
    another operation x2, other arithmetic, ensemble_weights(): return jax.scipy.linalg.cho_solve((factor, True), cross)  10.5 us
    mul x5, other arithmetic, net(): flow_z = coef_z * diff_z  7.78 us
    dot_general x1, matrix products, local(): jnp.dot(own_columns.T, lax.all_gather(scaled, 'grp', axis=0, tiled=True),...  7.11 us
  transfers between devices with their start and end apart: 14, of which 6 were waited for; matrix products, arithmetic and copies ran while one was open for 24% of the time, Pallas kernels for 0%

commit v1 on v0

--- a/solution.py
+++ b/solution.py
@@ -257,7 +257,16 @@
         axis=1,
     )
     slab_pred = cell_sum(picked, doubling=True)
-    predicted = lax.all_gather(slab_pred, "grp", axis=0, tiled=True)
+    ways = lax.axis_size("grp")
+    up = [(d, (d + 1) % ways) for d in range(ways)]
+    down = [(d, (d - 1) % ways) for d in range(ways)]
+    earlier, later = ([slab_pred], [slab_pred])
+    for _ in range(ways // 2):
+        earlier.append(lax.ppermute(earlier[-1], "grp", up))
+    for _ in range((ways - 1) // 2):
+        later.append(lax.ppermute(later[-1], "grp", down))
+    line = jnp.concatenate([*earlier[::-1], *later[1:]], axis=0)
+    predicted = jnp.roll(line, (lax.axis_index("grp") - ways // 2) * slab_pred.shape[0], axis=0)
     params = jnp.stack([log_perm, porosity], 1).reshape(local_members, 2 * cells_dev)
     offset = lax.axis_index("grp") * local_members
     own_columns = ensemble_weights(predicted, obs_values, obs_error, noise, offset, local_members)

time: 308 us -> 313 us (1.016); the launches traced: 308 us -> 309 us
  blocking collectives: 163 us -> 112 us
  starting transfers between devices: 27.4 us -> 75.1 us
  waiting for transfers between devices: 15 us -> 18.8 us
    all_gather x1 -> x0, blocking collectives: 50.4 us -> none  [local(): predicted = lax.all_gather(slab_pred, 'grp', axis=0, tiled=True)]
    ppermute x0 -> x7, starting transfers between devices: none -> 47.7 us  [the longest x4 44.4 us: local(): earlier.append(lax.ppermute(earlier[-1], 'grp', up))]
    ppermute x0 -> x7, waiting for transfers between devices: none -> 3.75 us  [the longest x4 2.93 us: local(): earlier.append(lax.ppermute(earlier[-1], 'grp', up))]
  transfers between devices with their start and end apart: 14 -> 21, of which waited for: 6 -> 13; matrix products, arithmetic and copies ran while one was open for 24% -> 24% of each run, Pallas kernels for 0% -> 0%
where the time goes in v1:
time: 313 us; the launch traced here: 309 us
  blocking collectives  112 us (36%)
  starting transfers between devices  75.1 us (24%)
  other arithmetic  64.8 us (21%)
  waiting for transfers between devices  18.8 us (6%)
  between operations  15.5 us (5%)
  local copies, waits for them, and re-layouts  12.5 us (4%)
  matrix products  9.88 us (3%)
    psum x10, blocking collectives, cell_sum(): values = lax.psum(values, axis)  112 us
    ppermute x4, starting transfers between devices, local(): earlier.append(lax.ppermute(earlier[-1], 'grp', up))  44.4 us
    ppermute x5, waiting for transfers between devices, cell_sum(): lax.ppermute(values, axis, [(i, i ^ step) for i in range(size)])  14.8 us
    another operation x3, other arithmetic, ensemble_weights(): factor = jnp.linalg.cholesky(gram)  12.4 us
    ppermute x3, starting transfers between devices, planes(): low = lax.ppermute(field[:, -1:], CELL, forward)  12.2 us
    another operation x2, other arithmetic, ensemble_weights(): return jax.scipy.linalg.cho_solve((factor, True), cross)  10.5 us
    mul x5, other arithmetic, net(): flow_z = coef_z * diff_z  7.72 us
    dot_general x1, matrix products, local(): jnp.dot(own_columns.T, lax.all_gather(scaled, 'grp', axis=0, tiled=True),...  7.11 us
  transfers between devices with their start and end apart: 21, of which 13 were waited for; matrix products, arithmetic and copies ran while one was open for 24% of the time, Pallas kernels for 0%

profile of v1, /device:TPU:1, one launch (start us, length us, event | category | flops | bytes accessed | tf_op | source)
XLA Modules:
  0.0 308.9 jit_solution(1426688836292358365)
XLA Ops:
  13.3 5.0 %collective-permute-start = (f32[16,3,1,16,128]{4,3,0,2,1:T(8,128)}, f32[16,3,1,16,128]{4,3,0,2,1:T(8,128)S(1)}, u32[]{:S(2)}, u32[]{:S(2)}) collective-permute-start(f32[16,3,1,16,128]{4,3,0,2,1:T(8,128)} %pad_maximum_fusion.12), channel_id=1, source_target_pairs={{0,1},{1,2},{2,3},{3,4},{4,5},{5,6},{6,7},{7,8},{8,9},{9,10},{10,1... | collective-permute-start | bytes 1179656 | tf_op jit(solution)/shard_map/ppermute | solution.py:163
  34.1 19.3 %psum.70 = f32[2,16]{1,0:T(2,128)S(1)} all-reduce(f32[2,16]{1,0:T(2,128)S(1)} %pad_maximum_fusion.16), channel_id=1, replica_groups=mesh['grp'=8,'cy'=4,'cz'=8] {'cz'}, use_global_device_ids=true, to_apply=%region_2.3 | all-reduce | flops 32 | bytes 256 | tf_op jit(solution)/shard_map/psum | solution.py:20
  53.5 10.2 %psum.71 = f32[2,16]{1,0:T(2,128)S(1)} all-reduce(f32[2,16]{1,0:T(2,128)S(1)} %psum.70), channel_id=1, replica_groups=mesh['grp'=8,'cy'=4,'cz'=8] {'cy'}, use_global_device_ids=true, to_apply=%region_3.4 | all-reduce | flops 32 | bytes 256 | tf_op jit(solution)/shard_map/psum | solution.py:20
  65.8 4.0 %collective-permute-start.3 = (f32[16,1,16,128]{3,2,1,0:T(8,128)S(1)}, f32[16,1,16,128]{3,2,1,0:T(8,128)S(1)}, u32[]{:S(2)}, u32[]{:S(2)}) collective-permute-start(f32[16,1,16,128]{3,2,1,0:T(8,128)S(1)} %get-tuple-element.72), channel_id=1, source_target_pairs={{0,1},{1,2},{2,3},{3,4},{4,5},{5,6},{6,7},{7,8},{8,9},{9,10},{10,1... | collective-permute-start | bytes 393224 | tf_op jit(solution)/shard_map/ppermute | solution.py:180
  76.6 14.2 %psum.72 = f32[3,16]{1,0:T(4,128)S(1)} all-reduce(f32[3,16]{1,0:T(4,128)S(1)} %pad_maximum_fusion.14), channel_id=1, replica_groups=mesh['grp'=8,'cy'=4,'cz'=8] {'cz'}, use_global_device_ids=true, to_apply=%region_7.8 | all-reduce | flops 48 | bytes 384 | tf_op jit(solution)/shard_map/psum | solution.py:20
  90.8 6.0 %psum.73 = f32[3,16]{1,0:T(4,128)S(1)} all-reduce(f32[3,16]{1,0:T(4,128)S(1)} %psum.72), channel_id=1, replica_groups=mesh['grp'=8,'cy'=4,'cz'=8] {'cy'}, use_global_device_ids=true, to_apply=%region_8.9 | all-reduce | flops 48 | bytes 384 | tf_op jit(solution)/shard_map/psum | solution.py:20
  97.5 2.6 multiply_subtract_fusion.1
  101.7 4.2 %collective-permute-start.5 = (f32[16,1,16,128]{3,2,1,0:T(8,128)S(1)}, f32[16,1,16,128]{3,2,1,0:T(8,128)S(1)}, u32[]{:S(2)}, u32[]{:S(2)}) collective-permute-start(f32[16,1,16,128]{3,2,1,0:T(8,128)S(1)} %get-tuple-element.70), channel_id=1, source_target_pairs={{0,1},{1,2},{2,3},{3,4},{4,5},{5,6},{6,7},{7,8},{8,9},{9,10},{10,1... | collective-permute-start | bytes 393224 | tf_op jit(solution)/shard_map/ppermute | solution.py:180
  112.2 14.7 %psum.74 = f32[4,16]{1,0:T(4,128)} all-reduce(f32[4,16]{1,0:T(4,128)S(1)} %pad_maximum_fusion.15), channel_id=1, replica_groups=mesh['grp'=8,'cy'=4,'cz'=8] {'cz'}, use_global_device_ids=true, to_apply=%region_13.14 | all-reduce | flops 64 | bytes 512 | tf_op jit(solution)/shard_map/psum | solution.py:20
  126.9 7.5 %psum.75 = f32[4,16]{1,0:T(4,128)} all-reduce(f32[4,16]{1,0:T(4,128)} %psum.74), channel_id=1, replica_groups=mesh['grp'=8,'cy'=4,'cz'=8] {'cy'}, use_global_device_ids=true, to_apply=%region_14.15 | all-reduce | flops 64 | bytes 512 | tf_op jit(solution)/shard_map/psum | solution.py:20
  136.1 2.4 copy_subtract_fusion
  140.4 4.0 %collective-permute-start.7 = (f32[16,1,16,128]{3,2,1,0:T(8,128)S(1)}, f32[16,1,16,128]{3,2,1,0:T(8,128)S(1)}, u32[]{:S(2)}, u32[]{:S(2)}) collective-permute-start(f32[16,1,16,128]{3,2,1,0:T(8,128)S(1)} %get-tuple-element.68), channel_id=1, source_target_pairs={{0,1},{1,2},{2,3},{3,4},{4,5},{5,6},{6,7},{7,8},{8,9},{9,10},{10,1... | collective-permute-start | bytes 393224 | tf_op jit(solution)/shard_map/ppermute | solution.py:180
  149.7 14.1 %psum.76 = f32[5,16]{1,0:T(8,128)S(1)} all-reduce(f32[5,16]{1,0:T(8,128)S(1)} %stack.169), channel_id=1, replica_groups=mesh['grp'=8,'cy'=4,'cz'=8] {'cz'}, use_global_device_ids=true, to_apply=%region_20.21 | all-reduce | flops 80 | bytes 640 | tf_op jit(solution)/shard_map/psum | solution.py:20
  163.8 7.9 %psum.77 = f32[5,16]{1,0:T(8,128)S(1)} all-reduce(f32[5,16]{1,0:T(8,128)S(1)} %psum.76), channel_id=1, replica_groups=mesh['grp'=8,'cy'=4,'cz'=8] {'cy'}, use_global_device_ids=true, to_apply=%region_21.22 | all-reduce | flops 80 | bytes 640 | tf_op jit(solution)/shard_map/psum | solution.py:20
  174.0 12.3 %psum.78 = f32[16]{0:T(128)S(1)} all-reduce(f32[16]{0:T(128)S(1)} %multiply_reduce_fusion.1), channel_id=1, replica_groups=mesh['grp'=8,'cy'=4,'cz'=8] {'cz'}, use_global_device_ids=true, to_apply=%region_23.24 | all-reduce | flops 16 | bytes 128 | tf_op jit(solution)/shard_map/psum | solution.py:20
  186.3 6.1 %psum.79 = f32[16]{0:T(128)S(1)} all-reduce(f32[16]{0:T(128)S(1)} %psum.78), channel_id=1, replica_groups=mesh['grp'=8,'cy'=4,'cz'=8] {'cy'}, use_global_device_ids=true, to_apply=%region_24.25 | all-reduce | flops 16 | bytes 128 | tf_op jit(solution)/shard_map/psum | solution.py:20
  197.8 2.5 collective-permute-done.8
  200.3 3.5 %collective-permute-done.9 = f32[16,256]{1,0:T(8,128)S(1)} collective-permute-done((f32[16,256]{1,0:T(8,128)S(1)}, f32[16,256]{1,0:T(8,128)S(1)}, u32[]{:S(2)}, u32[]{:S(2)}) %collective-permute-start.9) | collective-permute-done | bytes 16416 | tf_op jit(solution)/shard_map/ppermute | solution.py:24
  206.0 4.4 %collective-permute-done.10 = f32[16,256]{1,0:T(8,128)S(1)} collective-permute-done((f32[16,256]{1,0:T(8,128)S(1)}, f32[16,256]{1,0:T(8,128)S(1)}, u32[]{:S(2)}, u32[]{:S(2)}) %collective-permute-start.10) | collective-permute-done | bytes 16416 | tf_op jit(solution)/shard_map/ppermute | solution.py:24
  213.9 3.2 %collective-permute-done.12 = f32[16,256]{1,0:T(8,128)S(1)} collective-permute-done((f32[16,256]{1,0:T(8,128)S(1)}, f32[16,256]{1,0:T(8,128)S(1)}, u32[]{:S(2)}, u32[]{:S(2)}) %collective-permute-start.12) | collective-permute-done | bytes 16416 | tf_op jit(solution)/shard_map/ppermute | solution.py:24
  217.1 38.6 %collective-permute-start.13 = (f32[16,256]{1,0:T(8,128)S(1)}, f32[16,256]{1,0:T(8,128)S(1)}, u32[]{:S(2)}, u32[]{:S(2)}) collective-permute-start(f32[16,256]{1,0:T(8,128)S(1)} %add.491), channel_id=1, source_target_pairs={{0,32},{32,64},{64,96},{96,128},{128,160},{160,192},{192,224},{224... | collective-permute-start | bytes 49160 | tf_op jit(solution)/shard_map/ppermute | solution.py:265
  269.2 11.7 %cholesky.17 = f32[128,128]{1,0:T(8,128)S(1)} custom-call(f32[128,128]{1,0:T(8,128)S(1)} %fusion.71), custom_call_target="Cholesky" | custom-call | tf_op jit(solution)/shard_map/jit(cholesky)/cholesky | solution.py:138
  282.3 9.8 %custom-call.10 = f32[1,128,128]{1,2,0:T(8,128)S(1)} custom-call(f32[1,128,128]{2,1,0:T(8,128)S(1)} %fusion.65), custom_call_target="InvertDiagBlocksLowerTriangular" | custom-call | tf_op jit(solution)/shard_map/jit(_cho_solve)/triangular_solve | solution.py:139
  293.6 7.1 %fusion = f32[2,8,128,128]{3,1,2,0:T(8,128)S(1)} fusion(f32[128,16]{1,0:T(8,128)S(1)} %fusion.66, f32[128,16384]{1,0:T(8,128)} %all-gather.2.cloned.1.call-done, f32[2,8,128,128]{3,2,1,0:T(8,128)S(1)} %bitcast.504), kind=kOutput, calls=%fused_computation.3 | convolution fusion | flops 402915328 | bytes 10493952 | tf_op jit(solution)/shard_map/dot_general | solution.py:275
  (294 shorter events, 78.1 us)
Async XLA Ops:
  7.2 286.4 %all-gather.2.cloned.1.call-start = ((), (), s32[]{:S(2)}) async-start(), calls=%async_computation | async-start | bytes 9437184 | tf_op jit(solution)/shard_map/all_gather | solution.py:277
  11.3 15.3 %collective-permute-start.1 = (f32[16,3,1,16,128]{4,3,0,2,1:T(8,128)}, f32[16,3,1,16,128]{4,3,0,2,1:T(8,128)S(1)}, u32[]{:S(2)}, u32[]{:S(2)}) collective-permute-start(f32[16,3,1,16,128]{4,3,0,2,1:T(8,128)} %pad_maximum_fusion.13), channel_id=1, source_target_pairs={{1,0},{2,1},{3,2},{4,3},{5,4},{6,5},{7,6},{8,7},{9,8},{10,9},{11,1... | collective-permute-start | bytes 1179656 | tf_op jit(solution)/shard_map/ppermute | solution.py:164
  13.3 13.3 %collective-permute-start = (f32[16,3,1,16,128]{4,3,0,2,1:T(8,128)}, f32[16,3,1,16,128]{4,3,0,2,1:T(8,128)S(1)}, u32[]{:S(2)}, u32[]{:S(2)}) collective-permute-start(f32[16,3,1,16,128]{4,3,0,2,1:T(8,128)} %pad_maximum_fusion.12), channel_id=1, source_target_pairs={{0,1},{1,2},{2,3},{3,4},{4,5},{5,6},{6,7},{7,8},{8,9},{9,10},{10,1... | collective-permute-start | bytes 1179656 | tf_op jit(solution)/shard_map/ppermute | solution.py:163
  64.4 9.1 %collective-permute-start.2 = (f32[16,1,16,128]{3,2,1,0:T(8,128)S(1)}, f32[16,1,16,128]{3,2,1,0:T(8,128)S(1)}, u32[]{:S(2)}, u32[]{:S(2)}) collective-permute-start(f32[16,1,16,128]{3,2,1,0:T(8,128)S(1)} %get-tuple-element.71), channel_id=1, source_target_pairs={{1,0},{2,1},{3,2},{4,3},{5,4},{6,5},{7,6},{8,7},{9,8},{10,9},{11,1... | collective-permute-start | bytes 393224 | tf_op jit(solution)/shard_map/ppermute | solution.py:181
  65.8 7.7 %collective-permute-start.3 = (f32[16,1,16,128]{3,2,1,0:T(8,128)S(1)}, f32[16,1,16,128]{3,2,1,0:T(8,128)S(1)}, u32[]{:S(2)}, u32[]{:S(2)}) collective-permute-start(f32[16,1,16,128]{3,2,1,0:T(8,128)S(1)} %get-tuple-element.72), channel_id=1, source_target_pairs={{0,1},{1,2},{2,3},{3,4},{4,5},{5,6},{6,7},{7,8},{8,9},{9,10},{10,1... | collective-permute-start | bytes 393224 | tf_op jit(solution)/shard_map/ppermute | solution.py:180
  100.4 8.0 %collective-permute-start.4 = (f32[16,1,16,128]{3,2,1,0:T(8,128)S(1)}, f32[16,1,16,128]{3,2,1,0:T(8,128)S(1)}, u32[]{:S(2)}, u32[]{:S(2)}) collective-permute-start(f32[16,1,16,128]{3,2,1,0:T(8,128)S(1)} %get-tuple-element.69), channel_id=1, source_target_pairs={{1,0},{2,1},{3,2},{4,3},{5,4},{6,5},{7,6},{8,7},{9,8},{10,9},{11,1... | collective-permute-start | bytes 393224 | tf_op jit(solution)/shard_map/ppermute | solution.py:181
  101.7 6.7 %collective-permute-start.5 = (f32[16,1,16,128]{3,2,1,0:T(8,128)S(1)}, f32[16,1,16,128]{3,2,1,0:T(8,128)S(1)}, u32[]{:S(2)}, u32[]{:S(2)}) collective-permute-start(f32[16,1,16,128]{3,2,1,0:T(8,128)S(1)} %get-tuple-element.70), channel_id=1, source_target_pairs={{0,1},{1,2},{2,3},{3,4},{4,5},{5,6},{6,7},{7,8},{8,9},{9,10},{10,1... | collective-permute-start | bytes 393224 | tf_op jit(solution)/shard_map/ppermute | solution.py:180
  139.0 7.1 %collective-permute-start.6 = (f32[16,1,16,128]{3,2,1,0:T(8,128)S(1)}, f32[16,1,16,128]{3,2,1,0:T(8,128)S(1)}, u32[]{:S(2)}, u32[]{:S(2)}) collective-permute-start(f32[16,1,16,128]{3,2,1,0:T(8,128)S(1)} %get-tuple-element.67), channel_id=1, source_target_pairs={{1,0},{2,1},{3,2},{4,3},{5,4},{6,5},{7,6},{8,7},{9,8},{10,9},{11,1... | collective-permute-start | bytes 393224 | tf_op jit(solution)/shard_map/ppermute | solution.py:181
  140.4 5.9 %collective-permute-start.7 = (f32[16,1,16,128]{3,2,1,0:T(8,128)S(1)}, f32[16,1,16,128]{3,2,1,0:T(8,128)S(1)}, u32[]{:S(2)}, u32[]{:S(2)}) collective-permute-start(f32[16,1,16,128]{3,2,1,0:T(8,128)S(1)} %get-tuple-element.68), channel_id=1, source_target_pairs={{0,1},{1,2},{2,3},{3,4},{4,5},{5,6},{6,7},{7,8},{8,9},{9,10},{10,1... | collective-permute-start | bytes 393224 | tf_op jit(solution)/shard_map/ppermute | solution.py:180
  174.0 91.2 %copy-start.56 = (f32[256]{0:T(256)S(1)}, f32[256]{0:T(256)}, u32[]{:S(2)}) copy-start(f32[256]{0:T(256)} %param.16) | copy-start | bytes 3076
  192.6 99.5 %copy-start.57 = (f32[256]{0:T(256)S(1)}, f32[256]{0:T(256)}, u32[]{:S(2)}) copy-start(f32[256]{0:T(256)} %param.15) | copy-start | bytes 3076
  194.7 98.9 %copy-start.24 = (f32[16,2,4,16,128]{4,3,2,1,0:T(8,128)S(1)}, f32[16,2,4,16,128]{4,3,2,1,0:T(8,128)}, u32[]{:S(2)}) copy-start(f32[16,2,4,16,128]{4,3,2,1,0:T(8,128)} %copy-done.23) | copy-start | bytes 3145732
  197.6 2.7 collective-permute-start.8
  200.3 3.5 %collective-permute-start.9 = (f32[16,256]{1,0:T(8,128)S(1)}, f32[16,256]{1,0:T(8,128)S(1)}, u32[]{:S(2)}, u32[]{:S(2)}) collective-permute-start(f32[16,256]{1,0:T(8,128)S(1)} %add.487), channel_id=1, source_target_pairs={{0,2},{1,3},{2,0},{3,1},{4,6},{5,7},{6,4},{7,5},{8,10},{9,11},{10,... | collective-permute-start | bytes 49160 | tf_op jit(solution)/shard_map/ppermute | solution.py:24
  203.8 6.7 %collective-permute-start.10 = (f32[16,256]{1,0:T(8,128)S(1)}, f32[16,256]{1,0:T(8,128)S(1)}, u32[]{:S(2)}, u32[]{:S(2)}) collective-permute-start(f32[16,256]{1,0:T(8,128)S(1)} %add.488), channel_id=1, source_target_pairs={{0,4},{1,5},{2,6},{3,7},{4,0},{5,1},{6,2},{7,3},{8,12},{9,13},{10,... | collective-permute-start | bytes 49160 | tf_op jit(solution)/shard_map/ppermute | solution.py:24
  210.4 2.6 collective-permute-start.11
  213.0 4.1 %collective-permute-start.12 = (f32[16,256]{1,0:T(8,128)S(1)}, f32[16,256]{1,0:T(8,128)S(1)}, u32[]{:S(2)}, u32[]{:S(2)}) collective-permute-start(f32[16,256]{1,0:T(8,128)S(1)} %add.490), channel_id=1, source_target_pairs={{0,16},{8,24},{16,0},{24,8},{1,17},{9,25},{17,1},{25,9},{2,18},{10... | collective-permute-start | bytes 49160 | tf_op jit(solution)/shard_map/ppermute | solution.py:24
  217.1 39.4 %collective-permute-start.13 = (f32[16,256]{1,0:T(8,128)S(1)}, f32[16,256]{1,0:T(8,128)S(1)}, u32[]{:S(2)}, u32[]{:S(2)}) collective-permute-start(f32[16,256]{1,0:T(8,128)S(1)} %add.491), channel_id=1, source_target_pairs={{0,32},{32,64},{64,96},{96,128},{128,160},{160,192},{192,224},{224... | collective-permute-start | bytes 49160 | tf_op jit(solution)/shard_map/ppermute | solution.py:265
  256.6 3.2 %collective-permute-start.14 = (f32[16,256]{1,0:T(8,128)S(1)}, f32[16,256]{1,0:T(8,128)S(1)}, u32[]{:S(2)}, u32[]{:S(2)}) collective-permute-start(f32[16,256]{1,0:T(8,128)S(1)} %collective-permute-done.13), channel_id=1, source_target_pairs={{0,32},{32,64},{64,96},{96,128},{128,160},{160,192},{192,224},{224... | collective-permute-start | bytes 49160 | tf_op jit(solution)/shard_map/ppermute | solution.py:265
  258.9 3.5 %collective-permute-start.17 = (f32[16,256]{1,0:T(8,128)S(1)}, f32[16,256]{1,0:T(8,128)S(1)}, u32[]{:S(2)}, u32[]{:S(2)}) collective-permute-start(f32[16,256]{1,0:T(8,128)S(1)} %add.491), channel_id=1, source_target_pairs={{0,224},{32,0},{64,32},{96,64},{128,96},{160,128},{192,160},{224,1... | collective-permute-start | bytes 49160 | tf_op jit(solution)/shard_map/ppermute | solution.py:267
  259.7 4.3 %collective-permute-start.15 = (f32[16,256]{1,0:T(8,128)S(1)}, f32[16,256]{1,0:T(8,128)S(1)}, u32[]{:S(2)}, u32[]{:S(2)}) collective-permute-start(f32[16,256]{1,0:T(8,128)S(1)} %collective-permute-done.14), channel_id=1, source_target_pairs={{0,32},{32,64},{64,96},{96,128},{128,160},{160,192},{192,224},{224... | collective-permute-start | bytes 49160 | tf_op jit(solution)/shard_map/ppermute | solution.py:265
  262.3 3.2 %collective-permute-start.18 = (f32[16,256]{1,0:T(8,128)S(1)}, f32[16,256]{1,0:T(8,128)S(1)}, u32[]{:S(2)}, u32[]{:S(2)}) collective-permute-start(f32[16,256]{1,0:T(8,128)S(1)} %collective-permute-done.17), channel_id=1, source_target_pairs={{0,224},{32,0},{64,32},{96,64},{128,96},{160,128},{192,160},{224,1... | collective-permute-start | bytes 49160 | tf_op jit(solution)/shard_map/ppermute | solution.py:267
  264.0 4.4 %collective-permute-start.16 = (f32[16,256]{1,0:T(8,128)S(1)}, f32[16,256]{1,0:T(8,128)S(1)}, u32[]{:S(2)}, u32[]{:S(2)}) collective-permute-start(f32[16,256]{1,0:T(8,128)S(1)} %collective-permute-done.15), channel_id=1, source_target_pairs={{0,32},{32,64},{64,96},{96,128},{128,160},{160,192},{192,224},{224... | collective-permute-start | bytes 49160 | tf_op jit(solution)/shard_map/ppermute | solution.py:265
  265.5 3.2 %collective-permute-start.19 = (f32[16,256]{1,0:T(8,128)S(1)}, f32[16,256]{1,0:T(8,128)S(1)}, u32[]{:S(2)}, u32[]{:S(2)}) collective-permute-start(f32[16,256]{1,0:T(8,128)S(1)} %collective-permute-done.18), channel_id=1, source_target_pairs={{0,224},{32,0},{64,32},{96,64},{128,96},{160,128},{192,160},{224,1... | collective-permute-start | bytes 49160 | tf_op jit(solution)/shard_map/ppermute | solution.py:267
  (55 other events, 901.2 us)
Sparse Core Ops, SparseCore 0:
  22.7 56.6 all-gather.1
